TPU v7x, 512 devices: a whole 4x8x8 slice. The times are simulated.
512 devices in a mesh: head: 16 (over y, core), seq: 32 (over z, x).
Axes of the slice: x: 4, y: 8, z: 8, core: 2. Of those that a mesh axis runs over, the one named last changes fastest.
Arguments:
- queries: bfloat16 [32768, 2048], P(('seq', 'head'))
- keys: bfloat16 [32768, 2048], P(('seq', 'head'))
- values: bfloat16 [32768, 2048], P(('seq', 'head')), may hold values from -6 to 6
- grad_out: bfloat16 [32768, 2048], P(('seq', 'head')), may hold values from -6 to 6
- random_blocks: int32 [256, 3], P('seq'), may hold values from 0 to 255, as said below
Outputs:
- attended: bfloat16 [32768, 2048], P(('seq', 'head'))
- grad_queries: bfloat16 [32768, 2048], P(('seq', 'head'))
- grad_keys: bfloat16 [32768, 2048], P(('seq', 'head'))
- grad_values: bfloat16 [32768, 2048], P(('seq', 'head'))
Inputs may be any that keep to these rules, and one draw needn't show every extreme that they name: `random_blocks`: within the rows of one sequence group (8 consecutive query blocks), at most 2 entries name blocks of any one group's range of 8 blocks, and in every group's rows one group's range is named exactly 2 times.
All inputs are finite; a program needn't handle non-finite values.
Results may differ from a plain program's by a relative error of at most 0.022.
Values may be sent and summed in bfloat16 or wider, within the bound.
No kernel may reach another device: no remote copies, remote signals or barrier semaphores. Data moves between devices by JAX's collectives and lax.ppermute only.
A program may use at most 192 MiB of HBM per device.

v0:
```python
import jax
import jax.numpy as jnp
from jax import lax
from jax.sharding import PartitionSpec as P

HD = 128
BLK = 128
RAND = 3


def with_halo(cells, sides, width):
    for axis, dim in sides:
        count = lax.axis_size(axis)
        ends = count - 1
        head = lax.slice_in_dim(cells, 0, width, axis=dim)
        tail = lax.slice_in_dim(cells, cells.shape[dim] - width, cells.shape[dim], axis=dim)
        cells = jnp.concatenate(
            [
                lax.ppermute(tail, axis, [(i, (i + 1) % count) for i in range(ends)]),
                cells,
                lax.ppermute(head, axis, [((i + 1) % count, i) for i in range(ends)]),
            ],
            axis=dim,
        )
    return cells


def broadcast(value, axis):
    count = lax.axis_size(axis)
    me = lax.axis_index(axis)
    step = 1
    while step < count:
        pairs = [(i, i + step) for i in range(step) if i + step < count]
        got = lax.ppermute(value, axis, pairs)
        value = jnp.where((me >= step) & (me < 2 * step), got, value)
        step *= 2
    return value


def reduce_to_first(value, axis):
    count = lax.axis_size(axis)
    step = 1
    while step * 2 < count:
        step *= 2
    while step >= 1:
        pairs = [(i + step, i) for i in range(step) if i + step < count]
        value = value + lax.ppermute(value, axis, pairs)
        step //= 2
    return value


def slot_places(owners, groups, capacity):
    owner_hits = (owners[:, None] == jnp.arange(groups, dtype=jnp.int32)[None, :]).astype(jnp.int32)
    earlier = jnp.cumsum(owner_hits, axis=0) - owner_hits
    return owners * capacity + jnp.sum(earlier * owner_hits, axis=1)


def request_table(list_rows, query_count, groups, capacity):
    flat_rows = list_rows.reshape(-1)
    places = slot_places(flat_rows // query_count, groups, capacity)
    matches = places[None, :] == jnp.arange(groups * capacity, dtype=jnp.int32)[:, None]
    table = jnp.sum(jnp.where(matches, (flat_rows % query_count)[None, :], 0), axis=1)
    return table.reshape(groups, capacity)


def window_valid(my_group, query_count, groups):
    block_ids = jnp.arange(query_count, dtype=jnp.int32)
    left_ok = jnp.logical_not(jnp.logical_and(my_group == 0, block_ids == 0))
    right_ok = jnp.logical_not(
        jnp.logical_and(my_group == groups - 1, block_ids == query_count - 1)
    )
    all_true = jnp.ones((query_count, BLK), dtype=bool)
    return jnp.concatenate(
        [
            all_true,
            all_true,
            left_ok[:, None] & all_true,
            all_true,
            right_ok[:, None] & all_true,
            jnp.ones((query_count, RAND * BLK), dtype=bool),
        ],
        axis=1,
    )


def against_keys(rows, global_part, window_part, remote_part):
    return jnp.concatenate(
        [
            jnp.einsum("qihd,jhd->qhij", rows, global_part, preferred_element_type=jnp.float32),
            jnp.einsum("qihd,qjhd->qhij", rows, window_part, preferred_element_type=jnp.float32),
            jnp.einsum("qihd,qjhd->qhij", rows, remote_part, preferred_element_type=jnp.float32),
        ],
        axis=-1,
    )


def split_keys(table):
    return (table[..., : 2 * BLK], table[..., 2 * BLK : 5 * BLK], table[..., 5 * BLK :])


def weigh_keys(table, global_part, window_part, remote_part):
    global_w, window_w, random_w = split_keys(table)
    return (
        jnp.einsum("qhij,jhd->qihd", global_w, global_part, preferred_element_type=jnp.float32)
        + jnp.einsum("qhij,qjhd->qihd", window_w, window_part, preferred_element_type=jnp.float32)
        + jnp.einsum("qhij,qjhd->qihd", random_w, remote_part, preferred_element_type=jnp.float32)
    )


def key_terms(table, rows):
    global_w, window_w, random_w = split_keys(table)
    return (
        jnp.einsum("qhij,qihd->jhd", global_w, rows, preferred_element_type=jnp.float32),
        jnp.einsum("qhij,qihd->qjhd", window_w, rows, preferred_element_type=jnp.float32),
        jnp.einsum("qhij,qihd->qjhd", random_w, rows, preferred_element_type=jnp.float32),
    )


def shards(queries, keys, values, grad_out, random_blocks):
    groups = lax.axis_size("seq")
    my_group = lax.axis_index("seq")
    head_q, head_k, head_v, head_g = (
        lax.all_to_all(queries, "head", split_axis=1, concat_axis=0, tiled=True),
        lax.all_to_all(keys, "head", split_axis=1, concat_axis=0, tiled=True),
        lax.all_to_all(values, "head", split_axis=1, concat_axis=0, tiled=True),
        lax.all_to_all(grad_out, "head", split_axis=1, concat_axis=0, tiled=True),
    )
    group_tokens = head_q.shape[0]
    head_count = head_q.shape[1] // HD
    query_count = group_tokens // BLK
    capacity = max(2, 3 * query_count * RAND // (2 * groups))
    score_scale = HD ** (-0.5)
    key_value = jnp.stack([head_k, head_v])
    kv_blocks = key_value.reshape(2, query_count, BLK, head_count, HD)
    edged = with_halo(key_value, (("seq", 1),), BLK)
    edged = edged.reshape(2, query_count + 2, BLK, head_count, HD)
    window_kv = jnp.concatenate(
        [edged[:, 0:query_count], edged[:, 1 : query_count + 1], edged[:, 2 : query_count + 2]],
        axis=2,
    )
    global_kv = broadcast(kv_blocks[:, 0:2].reshape(2, 2 * BLK, head_count, HD), "seq")
    flat_ids = random_blocks.reshape(-1)
    places = slot_places(flat_ids // query_count, groups, capacity)
    wanted = lax.all_to_all(
        request_table(random_blocks, query_count, groups, capacity),
        "seq",
        split_axis=0,
        concat_axis=0,
        tiled=True,
    )
    served = jnp.take(kv_blocks, wanted.reshape(-1), axis=1)
    served = served.reshape(2, groups, capacity, BLK, head_count, HD)
    fetched = lax.all_to_all(served, "seq", split_axis=1, concat_axis=1, tiled=True)
    chosen = jnp.take(fetched.reshape(2, groups * capacity, BLK, head_count, HD), places, axis=1)
    remote_kv = chosen.reshape(2, query_count, RAND * BLK, head_count, HD)
    query_blocks = head_q.reshape(query_count, BLK, head_count, HD)
    grad_blocks = head_g.reshape(query_count, BLK, head_count, HD)
    scores = score_scale * against_keys(query_blocks, global_kv[0], window_kv[0], remote_kv[0])
    valid = window_valid(my_group, query_count, groups)
    scores = jnp.where(valid[:, None, None, :], scores, -jnp.inf)
    row_max = jnp.max(scores, axis=-1, keepdims=True)
    exponent = jnp.exp(scores - row_max)
    attention_probs = exponent / jnp.sum(exponent, axis=-1, keepdims=True)
    weights = attention_probs.astype(jnp.bfloat16)
    attended = weigh_keys(weights, global_kv[1], window_kv[1], remote_kv[1]).astype(jnp.bfloat16)
    grad_prob = against_keys(grad_blocks, global_kv[1], window_kv[1], remote_kv[1])
    row_delta = jnp.sum(attention_probs * grad_prob, axis=-1, keepdims=True)
    grad_score = (score_scale * attention_probs * (grad_prob - row_delta)).astype(jnp.bfloat16)
    grad_q = weigh_keys(grad_score, global_kv[0], window_kv[0], remote_kv[0]).astype(jnp.bfloat16)
    key_global, key_window, key_random = key_terms(grad_score, query_blocks)
    value_global, value_window, value_random = key_terms(weights, grad_blocks)
    global_sum = reduce_to_first(jnp.stack([key_global, value_global]), "seq")
    window_grad = jnp.stack([key_window, value_window]).reshape(
        2, query_count, 3, BLK, head_count, HD
    )
    no_pad = (0, 0)
    extended = (
        jnp.pad(window_grad[:, :, 0], (no_pad, (0, 2), no_pad, no_pad, no_pad))
        + jnp.pad(window_grad[:, :, 1], (no_pad, (1, 1), no_pad, no_pad, no_pad))
        + jnp.pad(window_grad[:, :, 2], (no_pad, (2, 0), no_pad, no_pad, no_pad))
    )
    outward = jnp.concatenate([extended[:, 0], extended[:, query_count + 1]], axis=1)
    inward = with_halo(outward.astype(jnp.bfloat16), (("seq", 1),), BLK).astype(outward.dtype)
    own_grad = extended[:, 1 : query_count + 1]
    own_grad = own_grad.at[:, 0].add(inward[:, :BLK])
    own_grad = own_grad.at[:, query_count - 1].add(inward[:, 3 * BLK :])
    random_terms = (
        jnp.stack([key_random, value_random])
        .reshape(2, query_count * RAND, BLK, head_count, HD)
        .astype(jnp.bfloat16)
    )
    send_pick = (places[None, :] == jnp.arange(groups * capacity, dtype=jnp.int32)[:, None]).astype(
        jnp.bfloat16
    )
    outgoing = jnp.einsum(
        "pj,xjihd->xpihd", send_pick, random_terms, preferred_element_type=jnp.float32
    ).astype(jnp.bfloat16)
    incoming = lax.all_to_all(
        outgoing.reshape(2, groups, capacity, BLK, head_count, HD),
        "seq",
        split_axis=1,
        concat_axis=1,
        tiled=True,
    )
    take_pick = (
        wanted.reshape(-1)[None, :] == jnp.arange(query_count, dtype=jnp.int32)[:, None]
    ).astype(jnp.bfloat16)
    random_sum = jnp.einsum(
        "qp,xpihd->xqihd",
        take_pick,
        incoming.reshape(2, groups * capacity, BLK, head_count, HD),
        preferred_element_type=jnp.float32,
    )
    global_sum = global_sum.reshape(2, 2, BLK, head_count, HD)
    own_grad = own_grad.at[:, 0:2].add(jnp.where(my_group == 0, global_sum, 0.0))
    total_grad = own_grad + random_sum
    grad_k = total_grad[0].reshape(group_tokens, head_count * HD).astype(jnp.bfloat16)
    grad_v = total_grad[1].reshape(group_tokens, head_count * HD).astype(jnp.bfloat16)
    return (
        lax.all_to_all(
            attended.reshape(group_tokens, head_count * HD),
            "head",
            split_axis=0,
            concat_axis=1,
            tiled=True,
        ),
        lax.all_to_all(
            grad_q.reshape(group_tokens, head_count * HD),
            "head",
            split_axis=0,
            concat_axis=1,
            tiled=True,
        ),
        lax.all_to_all(grad_k, "head", split_axis=0, concat_axis=1, tiled=True),
        lax.all_to_all(grad_v, "head", split_axis=0, concat_axis=1, tiled=True),
    )


def solution(mesh):
    placed = (
        P(("seq", "head"), None),
        P(("seq", "head"), None),
        P(("seq", "head"), None),
        P(("seq", "head"), None),
        P("seq", None),
    )
    return jax.shard_map(
        shards,
        mesh=mesh,
        in_specs=placed,
        out_specs=(
            P(("seq", "head"), None),
            P(("seq", "head"), None),
            P(("seq", "head"), None),
            P(("seq", "head"), None),
        ),
        check_vma=False,
    )
```

profile of v0, /device:TPU:3, one launch (start us, length us, event | category | flops | bytes accessed | tf_op | source)
XLA Modules:
  0.0 459.8 jit_solution(10940676813869439960)
XLA Ops:
  2.7 12.9 %all-to-all-start.3 = ((s32[32,1,2]{2,1,0:T(1,128)}), s32[32,1,2]{2,1,0:T(1,128)S(1)}, u32[]{:S(2)}, u32[]{:S(2)}) async-start(s32[32,1,2]{2,1,0:T(1,128)} %bitcast.20), calls=%async_computation.3 | async-start | bytes 32768 | tf_op jit(solution)/shard_map/all_to_all | solution.py:144
  16.4 6.8 %all-to-all-done.3 = s32[32,1,2]{2,1,0:T(1,128)S(1)} async-done(((s32[32,1,2]{2,1,0:T(1,128)}), s32[32,1,2]{2,1,0:T(1,128)S(1)}, u32[]{:S(2)}, u32[]{:S(2)}) %all-to-all-start.3) | async-done | bytes 288 | tf_op jit(solution)/shard_map/all_to_all | solution.py:144
  23.2 9.2 %all-to-all-start.2 = ((bf16[64,16,128]{2,0,1:T(8,128)(2,1)}), bf16[64,16,128]{2,0,1:T(8,128)(2,1)S(1)}, u32[]{:S(2)}, u32[]{:S(2)}) async-start(bf16[64,16,128]{2,0,1:T(8,128)(2,1)} %copy_bitcast_fusion.8), calls=%async_computation.2 | async-start | bytes 524288 | tf_op jit(solution)/shard_map/all_to_all | solution.py:123
  32.4 1.7 copy_bitcast_fusion.10
  34.2 10.0 %all-to-all-done.2 = bf16[64,16,128]{2,0,1:T(8,128)(2,1)S(1)} async-done(((bf16[64,16,128]{2,0,1:T(8,128)(2,1)}), bf16[64,16,128]{2,0,1:T(8,128)(2,1)S(1)}, u32[]{:S(2)}, u32[]{:S(2)}) %all-to-all-start.2) | async-done | bytes 262176 | tf_op jit(solution)/shard_map/all_to_all | solution.py:123
  44.1 3.4 all-to-all-start
  50.5 8.2 %all-to-all-done = bf16[64,16,128]{2,0,1:T(8,128)(2,1)S(1)} async-done(((bf16[64,16,128]{2,0,1:T(8,128)(2,1)}), bf16[64,16,128]{2,0,1:T(8,128)(2,1)S(1)}, u32[]{:S(2)}, u32[]{:S(2)}) %all-to-all-start) | async-done | bytes 262176 | tf_op jit(solution)/shard_map/all_to_all | solution.py:124
  58.7 3.4 all-to-all-start.1
  62.3 11.6 %all-to-all-done.1 = bf16[64,16,128]{2,0,1:T(8,128)(2,1)S(1)} async-done(((bf16[64,16,128]{2,0,1:T(8,128)(2,1)}), bf16[64,16,128]{2,0,1:T(8,128)(2,1)S(1)}, u32[]{:S(2)}, u32[]{:S(2)}) %all-to-all-start.1) | async-done | bytes 262176 | tf_op jit(solution)/shard_map/all_to_all | solution.py:125
  73.8 3.4 all-to-all-start.6
  77.3 3.1 gather_fusion
  80.4 2.7 copy.169
  83.6 2.5 copy.170
  86.1 2.3 all-to-all-done.6
  88.4 5.6 %all-to-all-start.4 = ((bf16[2,32,2,128,1,128]{5,3,2,0,4,1:T(8,128)(2,1)}), bf16[2,32,2,128,1,128]{5,3,2,0,4,1:T(8,128)(2,1)}, u32[]{:S(2)}, u32[]{:S(2)}) async-start(bf16[2,32,2,128,1,128]{5,3,2,0,4,1:T(8,128)(2,1)} %copy.170), calls=%async_computation.4 | async-start | bytes 8388608 | tf_op jit(solution)/shard_map/all_to_all | solution.py:153
  94.4 3.1 collective-permute-start.5
  97.5 2.2 collective-permute-start.6
  101.0 7.7 %collective-permute-done.5 = bf16[2,128,128]{2,1,0:T(8,128)(2,1)S(1)} collective-permute-done((bf16[2,128,128]{2,1,0:T(8,128)(2,1)S(1)}, bf16[2,128,128]{2,1,0:T(8,128)(2,1)S(1)}, u32[]{:S(2)}, u32[]{:S(2)}) %collective-permute-start.5) | collective-permute-done | bytes 65568 | tf_op jit(solution)/shard_map/ppermute | solution.py:19
  108.7 3.4 collective-permute-done
  112.1 78.6 %collective-permute-start.1 = (bf16[2,256,1,128]{3,1,2,0:T(8,128)(2,1)S(1)}, bf16[2,256,1,128]{3,1,2,0:T(8,128)(2,1)S(1)}, u32[]{:S(2)}, u32[]{:S(2)}) collective-permute-start(bf16[2,256,1,128]{3,1,2,0:T(8,128)(2,1)S(1)} %broadcast_select_fusion.1), channel_id=1, source_target_pairs={{0,2},{1,3},{32,34},{33,35},{64,66},{65,67},{96,98},{97,99},{128,1... | collective-permute-start | bytes 393224 | tf_op jit(solution)/shard_map/ppermute | solution.py:34
  191.1 1.6 collective-permute-done.1
  194.1 1.8 collective-permute-done.2
  197.6 1.6 collective-permute-done.3
  204.7 4.8 %copy.171 = bf16[2,32,2,128,1,128]{5,3,2,1,0,4:T(8,128)(2,1)} copy(bf16[2,32,2,128,1,128]{5,3,2,0,4,1:T(8,128)(2,1)} %all-to-all-done.4) | data formatting | bytes 8388608 | tf_op jit(solution)/shard_map/all_to_all | solution.py:153
  209.5 4.1 gather_fusion.1
  213.6 1.6 bitcast_select_fusion
  220.4 1.9 multiply_reduce_fusion
  222.3 2.3 multiply_convert_fusion
  228.6 6.7 %copy.190 = bf16[2,32,2,128,1,128]{5,2,3,0,4,1:T(2,128)(2,1)} copy(bf16[2,32,2,128,1,128]{5,2,1,3,0,4:T(2,128)(2,1)S(1)} %bitcast.311) | data formatting | bytes 8388608 | tf_op jit(solution)/shard_map/reshape | solution.py:199
  235.3 17.6 %all-to-all-start.8 = ((bf16[2,32,2,128,1,128]{5,2,3,0,4,1:T(2,128)(2,1)}), bf16[2,32,2,128,1,128]{5,2,3,0,4,1:T(2,128)(2,1)}, u32[]{:S(2)}, u32[]{:S(2)}) async-start(bf16[2,32,2,128,1,128]{5,2,3,0,4,1:T(2,128)(2,1)} %copy.190), calls=%async_computation.8 | async-start | bytes 8388608 | tf_op jit(solution)/shard_map/all_to_all | solution.py:198
  259.9 93.3 %collective-permute-done.9 = f32[2,256,1,128]{3,1,2,0:T(8,128)S(1)} collective-permute-done((f32[2,256,1,128]{3,1,2,0:T(8,128)S(1)}, f32[2,256,1,128]{3,1,2,0:T(8,128)S(1)}, u32[]{:S(2)}, u32[]{:S(2)}) %collective-permute-start.9) | collective-permute-done | bytes 262176 | tf_op jit(solution)/shard_map/ppermute | solution.py:47
  355.1 3.5 collective-permute-start.7
  358.6 1.9 collective-permute-start.8
  361.0 5.7 %collective-permute-done.10 = f32[2,256,1,128]{3,1,2,0:T(8,128)S(1)} collective-permute-done((f32[2,256,1,128]{3,1,2,0:T(8,128)S(1)}, f32[2,256,1,128]{3,1,2,0:T(8,128)S(1)}, u32[]{:S(2)}, u32[]{:S(2)}) %collective-permute-start.10) | collective-permute-done | bytes 262176 | tf_op jit(solution)/shard_map/ppermute | solution.py:47
  369.1 5.5 %collective-permute-done.11 = f32[2,256,1,128]{3,1,2,0:T(8,128)S(1)} collective-permute-done((f32[2,256,1,128]{3,1,2,0:T(8,128)S(1)}, f32[2,256,1,128]{3,1,2,0:T(8,128)S(1)}, u32[]{:S(2)}, u32[]{:S(2)}) %collective-permute-start.11) | collective-permute-done | bytes 262176 | tf_op jit(solution)/shard_map/ppermute | solution.py:47
  377.0 6.3 %collective-permute-done.12 = f32[2,256,1,128]{3,1,2,0:T(8,128)S(1)} collective-permute-done((f32[2,256,1,128]{3,1,2,0:T(8,128)S(1)}, f32[2,256,1,128]{3,1,2,0:T(8,128)S(1)}, u32[]{:S(2)}, u32[]{:S(2)}) %collective-permute-start.12) | collective-permute-done | bytes 262176 | tf_op jit(solution)/shard_map/ppermute | solution.py:47
  383.3 3.4 collective-permute-start.13
  387.5 3.0 scatter-add.11
  390.5 10.5 %all-to-all-start.5 = ((bf16[16,64,128]{2,1,0:T(8,128)(2,1)}), bf16[16,64,128]{2,1,0:T(8,128)(2,1)S(1)}, u32[]{:S(2)}, u32[]{:S(2)}) async-start(bf16[16,64,128]{2,1,0:T(8,128)(2,1)} %bitcast.45), calls=%async_computation.5 | async-start | bytes 524288 | tf_op jit(solution)/shard_map/all_to_all | solution.py:220
  401.4 9.0 %copy.191 = bf16[2,32,2,128,1,128]{5,2,1,3,0,4:T(2,128)(2,1)} copy(bf16[2,32,2,128,1,128]{5,2,3,0,4,1:T(2,128)(2,1)} %all-to-all-done.8) | data formatting | bytes 8388608 | tf_op jit(solution)/shard_map/all_to_all | solution.py:198
  410.4 2.5 all-to-all-done.5
  412.9 4.8 %all-to-all-start.7 = ((bf16[16,64,128]{2,1,0:T(8,128)(2,1)}), bf16[16,64,128]{2,1,0:T(8,128)(2,1)S(1)}, u32[]{:S(2)}, u32[]{:S(2)}) async-start(bf16[16,64,128]{2,1,0:T(8,128)(2,1)} %bitcast.67), calls=%async_computation.7 | async-start | bytes 524288 | tf_op jit(solution)/shard_map/all_to_all | solution.py:227
  417.7 2.8 fusion.7
  421.3 8.1 %all-to-all-done.7 = bf16[16,64,128]{2,1,0:T(8,128)(2,1)S(1)} async-done(((bf16[16,64,128]{2,1,0:T(8,128)(2,1)}), bf16[16,64,128]{2,1,0:T(8,128)(2,1)S(1)}, u32[]{:S(2)}, u32[]{:S(2)}) %all-to-all-start.7) | async-done | bytes 262176 | tf_op jit(solution)/shard_map/all_to_all | solution.py:227
  429.4 3.4 all-to-all-start.10
  434.3 9.6 %all-to-all-done.10 = bf16[16,64,128]{2,1,0:T(8,128)(2,1)S(1)} async-done(((bf16[16,64,128]{2,1,0:T(8,128)(2,1)}), bf16[16,64,128]{2,1,0:T(8,128)(2,1)S(1)}, u32[]{:S(2)}, u32[]{:S(2)}) %all-to-all-start.10) | async-done | bytes 262176 | tf_op jit(solution)/shard_map/all_to_all | solution.py:235
  443.9 3.4 all-to-all-start.9
  448.8 10.2 %all-to-all-done.9 = bf16[16,64,128]{2,1,0:T(8,128)(2,1)S(1)} async-done(((bf16[16,64,128]{2,1,0:T(8,128)(2,1)}), bf16[16,64,128]{2,1,0:T(8,128)(2,1)S(1)}, u32[]{:S(2)}, u32[]{:S(2)}) %all-to-all-start.9) | async-done | bytes 262176 | tf_op jit(solution)/shard_map/all_to_all | solution.py:234
  (145 shorter events, 45.6 us)
Async XLA Ops:
  0.6 15.0 %copy-start = (bf16[64,2048]{1,0:T(8,128)(2,1)S(1)}, bf16[64,2048]{1,0:T(8,128)(2,1)}, u32[]{:S(2)}) copy-start(bf16[64,2048]{1,0:T(8,128)(2,1)} %param.11) | copy-start | bytes 786436
  0.6 46.9 %copy-start.16 = (bf16[64,2048]{1,0:T(8,128)(2,1)S(1)}, bf16[64,2048]{1,0:T(8,128)(2,1)}, u32[]{:S(2)}) copy-start(bf16[64,2048]{1,0:T(8,128)(2,1)} %param.13) | copy-start | bytes 786436
  0.7 47.7 %copy-start.17 = (bf16[64,2048]{1,0:T(8,128)(2,1)S(1)}, bf16[64,2048]{1,0:T(8,128)(2,1)}, u32[]{:S(2)}) copy-start(bf16[64,2048]{1,0:T(8,128)(2,1)} %param.14) | copy-start | bytes 786436
  2.7 20.5 %all-to-all-start.3 = ((s32[32,1,2]{2,1,0:T(1,128)}), s32[32,1,2]{2,1,0:T(1,128)S(1)}, u32[]{:S(2)}, u32[]{:S(2)}) async-start(s32[32,1,2]{2,1,0:T(1,128)} %bitcast.20), calls=%async_computation.3 | async-start | bytes 32768 | tf_op jit(solution)/shard_map/all_to_all | solution.py:144
  23.2 20.9 %all-to-all-start.2 = ((bf16[64,16,128]{2,0,1:T(8,128)(2,1)}), bf16[64,16,128]{2,0,1:T(8,128)(2,1)S(1)}, u32[]{:S(2)}, u32[]{:S(2)}) async-start(bf16[64,16,128]{2,0,1:T(8,128)(2,1)} %copy_bitcast_fusion.8), calls=%async_computation.2 | async-start | bytes 524288 | tf_op jit(solution)/shard_map/all_to_all | solution.py:123
  44.1 14.6 %all-to-all-start = ((bf16[64,16,128]{2,0,1:T(8,128)(2,1)}), bf16[64,16,128]{2,0,1:T(8,128)(2,1)S(1)}, u32[]{:S(2)}, u32[]{:S(2)}) async-start(bf16[64,16,128]{2,0,1:T(8,128)(2,1)} %copy_bitcast_fusion.10), calls=%async_computation | async-start | bytes 524288 | tf_op jit(solution)/shard_map/all_to_all | solution.py:124
  58.7 15.1 %all-to-all-start.1 = ((bf16[64,16,128]{2,0,1:T(8,128)(2,1)}), bf16[64,16,128]{2,0,1:T(8,128)(2,1)S(1)}, u32[]{:S(2)}, u32[]{:S(2)}) async-start(bf16[64,16,128]{2,0,1:T(8,128)(2,1)} %copy_bitcast_fusion.9), calls=%async_computation.1 | async-start | bytes 524288 | tf_op jit(solution)/shard_map/all_to_all | solution.py:125
  73.8 14.5 %all-to-all-start.6 = ((bf16[64,16,128]{2,0,1:T(8,128)(2,1)}), bf16[64,16,128]{2,0,1:T(8,128)(2,1)S(1)}, u32[]{:S(2)}, u32[]{:S(2)}) async-start(bf16[64,16,128]{2,0,1:T(8,128)(2,1)} %copy_bitcast_fusion.7), calls=%async_computation.6 | async-start | bytes 524288 | tf_op jit(solution)/shard_map/all_to_all | solution.py:126
  88.4 116.3 %all-to-all-start.4 = ((bf16[2,32,2,128,1,128]{5,3,2,0,4,1:T(8,128)(2,1)}), bf16[2,32,2,128,1,128]{5,3,2,0,4,1:T(8,128)(2,1)}, u32[]{:S(2)}, u32[]{:S(2)}) async-start(bf16[2,32,2,128,1,128]{5,3,2,0,4,1:T(8,128)(2,1)} %copy.170), calls=%async_computation.4 | async-start | bytes 8388608 | tf_op jit(solution)/shard_map/all_to_all | solution.py:153
  94.4 14.3 %collective-permute-start.5 = (bf16[2,128,128]{2,1,0:T(8,128)(2,1)S(1)}, bf16[2,128,128]{2,1,0:T(8,128)(2,1)S(1)}, u32[]{:S(2)}, u32[]{:S(2)}) collective-permute-start(bf16[2,128,128]{2,1,0:T(8,128)(2,1)S(1)} %get-tuple-element.58), channel_id=1, source_target_pairs={{0,1},{1,2},{2,3},{3,4},{4,5},{5,6},{6,7},{7,8},{8,9},{9,10},{10,1... | collective-permute-start | bytes 196616 | tf_op jit(solution)/shard_map/ppermute | solution.py:19
  97.5 11.2 %collective-permute-start.6 = (bf16[2,128,128]{2,1,0:T(8,128)(2,1)S(1)}, bf16[2,128,128]{2,1,0:T(8,128)(2,1)S(1)}, u32[]{:S(2)}, u32[]{:S(2)}) collective-permute-start(bf16[2,128,128]{2,1,0:T(8,128)(2,1)S(1)} %get-tuple-element.59), channel_id=1, source_target_pairs={{1,0},{2,1},{3,2},{4,3},{5,4},{6,5},{7,6},{8,7},{9,8},{10,9},{11,1... | collective-permute-start | bytes 196616 | tf_op jit(solution)/shard_map/ppermute | solution.py:21
  99.7 12.4 %collective-permute-start = (bf16[2,256,1,128]{3,1,2,0:T(8,128)(2,1)S(1)}, bf16[2,256,1,128]{3,1,2,0:T(8,128)(2,1)S(1)}, u32[]{:S(2)}, u32[]{:S(2)}) collective-permute-start(bf16[2,256,1,128]{3,1,2,0:T(8,128)(2,1)S(1)} %bitcast.347), channel_id=1, source_target_pairs={{0,1},{32,33},{64,65},{96,97},{128,129},{160,161},{192,193},{224,2... | collective-permute-start | bytes 393224 | tf_op jit(solution)/shard_map/ppermute | solution.py:34
  112.1 80.5 %collective-permute-start.1 = (bf16[2,256,1,128]{3,1,2,0:T(8,128)(2,1)S(1)}, bf16[2,256,1,128]{3,1,2,0:T(8,128)(2,1)S(1)}, u32[]{:S(2)}, u32[]{:S(2)}) collective-permute-start(bf16[2,256,1,128]{3,1,2,0:T(8,128)(2,1)S(1)} %broadcast_select_fusion.1), channel_id=1, source_target_pairs={{0,2},{1,3},{32,34},{33,35},{64,66},{65,67},{96,98},{97,99},{128,1... | collective-permute-start | bytes 393224 | tf_op jit(solution)/shard_map/ppermute | solution.py:34
  192.6 3.2 collective-permute-start.2
  194.1 8.1 %copy-start.6 = (bf16[2,8,384,1,128]{4,2,1,3,0:T(8,128)(2,1)}, bf16[2,8,384,1,128]{4,2,1,3,0:T(8,128)(2,1)S(1)}, u32[]{:S(2)}) copy-start(bf16[2,8,384,1,128]{4,2,1,3,0:T(8,128)(2,1)S(1)} %pad_maximum_fusion.1) | copy-start | bytes 4718596
  195.9 3.3 collective-permute-start.3
  199.2 3.8 collective-permute-start.4
  215.4 1.8 copy-start.10
  215.4 3.3 copy-start.12
  218.7 1.4 copy-start.8
  218.7 1.7 copy-start.9
  224.7 1.4 copy-start.2
  224.7 2.0 copy-start.4
  235.3 17.7 %copy-start.3 = (bf16[8,1,128,1024]{2,3,0,1:T(8,128)(2,1)S(1)}, bf16[8,1,128,1024]{2,3,0,1:T(8,128)(2,1)}, u32[]{:S(2)}) copy-start(bf16[8,1,128,1024]{2,3,0,1:T(8,128)(2,1)} %copy-done.2) | copy-start | bytes 6291460
  235.3 155.3 %all-to-all-start.8 = ((bf16[2,32,2,128,1,128]{5,2,3,0,4,1:T(2,128)(2,1)}), bf16[2,32,2,128,1,128]{5,2,3,0,4,1:T(2,128)(2,1)}, u32[]{:S(2)}, u32[]{:S(2)}) async-start(bf16[2,32,2,128,1,128]{5,2,3,0,4,1:T(2,128)(2,1)} %copy.190), calls=%async_computation.8 | async-start | bytes 8388608 | tf_op jit(solution)/shard_map/all_to_all | solution.py:198
  253.2 3.4 copy-start.5
  254.8 98.5 %collective-permute-start.9 = (f32[2,256,1,128]{3,1,2,0:T(8,128)S(1)}, f32[2,256,1,128]{3,1,2,0:T(8,128)S(1)}, u32[]{:S(2)}, u32[]{:S(2)}) collective-permute-start(f32[2,256,1,128]{3,1,2,0:T(8,128)S(1)} %pad_maximum_fusion.5), channel_id=1, source_target_pairs={{16,0},{17,1},{18,2},{19,3},{20,4},{21,5},{22,6},{23,7},{24,8},{25... | collective-permute-start | bytes 786440 | tf_op jit(solution)/shard_map/ppermute | solution.py:47
  257.4 1.1 copy-start.13
  257.4 1.7 copy-start.7
  259.7 94.9 %copy-start.11 = (bf16[1,24,128,1,128]{4,2,0,1,3:T(8,128)(2,1)S(1)}, bf16[1,24,128,1,128]{4,2,0,1,3:T(8,128)(2,1)}, u32[]{:S(2)}) copy-start(bf16[1,24,128,1,128]{4,2,0,1,3:T(8,128)(2,1)} %copy-done.10) | copy-start | bytes 2359300
  259.9 95.2 %copy-start.14 = (f32[2,10,128,1,128]{4,2,0,3,1:T(8,128)}, f32[2,10,128,1,128]{4,2,0,3,1:T(8,128)S(1)}, u32[]{:S(2)}) copy-start(f32[2,10,128,1,128]{4,2,0,3,1:T(8,128)S(1)} %bitcast_add_fusion) | copy-start | bytes 3932164
  353.3 13.4 %collective-permute-start.10 = (f32[2,256,1,128]{3,1,2,0:T(8,128)S(1)}, f32[2,256,1,128]{3,1,2,0:T(8,128)S(1)}, u32[]{:S(2)}, u32[]{:S(2)}) collective-permute-start(f32[2,256,1,128]{3,1,2,0:T(8,128)S(1)} %fusion.39), channel_id=1, source_target_pairs={{8,0},{9,1},{10,2},{11,3},{12,4},{13,5},{14,6},{15,7},{40,32},{41,... | collective-permute-start | bytes 786440 | tf_op jit(solution)/shard_map/ppermute | solution.py:47
  355.1 31.6 %collective-permute-start.7 = (bf16[2,128,1,128]{3,1,0,2:T(8,128)(2,1)S(1)}, bf16[2,128,1,128]{3,1,0,2:T(8,128)(2,1)S(1)}, u32[]{:S(2)}, u32[]{:S(2)}) collective-permute-start(bf16[2,128,1,128]{3,1,0,2:T(8,128)(2,1)S(1)} %get-tuple-element.49), channel_id=1, source_target_pairs={{0,1},{1,2},{2,3},{3,4},{4,5},{5,6},{6,7},{7,8},{8,9},{9,10},{10,1... | collective-permute-start | bytes 196616 | tf_op jit(solution)/shard_map/ppermute | solution.py:19
  358.6 28.1 %collective-permute-start.8 = (bf16[2,128,1,128]{3,1,0,2:T(8,128)(2,1)S(1)}, bf16[2,128,1,128]{3,1,0,2:T(8,128)(2,1)S(1)}, u32[]{:S(2)}, u32[]{:S(2)}) collective-permute-start(bf16[2,128,1,128]{3,1,0,2:T(8,128)(2,1)S(1)} %get-tuple-element.50), channel_id=1, source_target_pairs={{1,0},{2,1},{3,2},{4,3},{5,4},{6,5},{7,6},{8,7},{9,8},{10,9},{11,1... | collective-permute-start | bytes 196616 | tf_op jit(solution)/shard_map/ppermute | solution.py:21
  366.8 7.9 %collective-permute-start.11 = (f32[2,256,1,128]{3,1,2,0:T(8,128)S(1)}, f32[2,256,1,128]{3,1,2,0:T(8,128)S(1)}, u32[]{:S(2)}, u32[]{:S(2)}) collective-permute-start(f32[2,256,1,128]{3,1,2,0:T(8,128)S(1)} %fusion.61), channel_id=1, source_target_pairs={{4,0},{5,1},{6,2},{7,3},{36,32},{37,33},{38,34},{39,35},{68,64},{6... | collective-permute-start | bytes 786440 | tf_op jit(solution)/shard_map/ppermute | solution.py:47
  369.1 17.6 %copy-start.15 = (f32[2,10,128,1,128]{4,2,0,3,1:T(8,128)S(1)}, f32[2,10,128,1,128]{4,2,0,3,1:T(8,128)}, u32[]{:S(2)}) copy-start(f32[2,10,128,1,128]{4,2,0,3,1:T(8,128)} %copy-done.14) | copy-start | bytes 3932164
  369.1 17.6 %slice-start = ((f32[2,10,128,1,128]{4,2,0,3,1:T(8,128)}), f32[2,8,128,1,128]{4,2,0,3,1:T(8,128)S(1)}, s32[]{:S(2)}) async-start(f32[2,10,128,1,128]{4,2,0,3,1:T(8,128)} %copy-done.14), calls=%async_computation.11 | async-start | bytes 2097152 | tf_op jit(solution)/shard_map/slice | solution.py:184
  374.6 8.6 %collective-permute-start.12 = (f32[2,256,1,128]{3,1,2,0:T(8,128)S(1)}, f32[2,256,1,128]{3,1,2,0:T(8,128)S(1)}, u32[]{:S(2)}, u32[]{:S(2)}) collective-permute-start(f32[2,256,1,128]{3,1,2,0:T(8,128)S(1)} %add.165), channel_id=1, source_target_pairs={{2,0},{3,1},{34,32},{35,33},{66,64},{67,65},{98,96},{99,97},{130,1... | collective-permute-start | bytes 786440 | tf_op jit(solution)/shard_map/ppermute | solution.py:47
  383.3 17.7 %collective-permute-start.13 = (f32[2,256,1,128]{3,1,2,0:T(8,128)S(1)}, f32[2,256,1,128]{3,1,2,0:T(8,128)S(1)}, u32[]{:S(2)}, u32[]{:S(2)}) collective-permute-start(f32[2,256,1,128]{3,1,2,0:T(8,128)S(1)} %add.166), channel_id=1, source_target_pairs={{1,0},{33,32},{65,64},{97,96},{129,128},{161,160},{193,192},{225,2... | collective-permute-start | bytes 786440 | tf_op jit(solution)/shard_map/ppermute | solution.py:47
  390.5 22.4 %all-to-all-start.5 = ((bf16[16,64,128]{2,1,0:T(8,128)(2,1)}), bf16[16,64,128]{2,1,0:T(8,128)(2,1)S(1)}, u32[]{:S(2)}, u32[]{:S(2)}) async-start(bf16[16,64,128]{2,1,0:T(8,128)(2,1)} %bitcast.45), calls=%async_computation.5 | async-start | bytes 524288 | tf_op jit(solution)/shard_map/all_to_all | solution.py:220
  412.9 16.5 %all-to-all-start.7 = ((bf16[16,64,128]{2,1,0:T(8,128)(2,1)}), bf16[16,64,128]{2,1,0:T(8,128)(2,1)S(1)}, u32[]{:S(2)}, u32[]{:S(2)}) async-start(bf16[16,64,128]{2,1,0:T(8,128)(2,1)} %bitcast.67), calls=%async_computation.7 | async-start | bytes 524288 | tf_op jit(solution)/shard_map/all_to_all | solution.py:227
  420.5 39.3 %copy-start.1 = (bf16[64,2048]{1,0:T(8,128)(2,1)S(1)}, bf16[64,2048]{1,0:T(8,128)(2,1)}, u32[]{:S(2)}) copy-start(bf16[64,2048]{1,0:T(8,128)(2,1)} %param.11) | copy-start | bytes 786436
  429.4 14.6 %all-to-all-start.10 = ((bf16[16,64,128]{2,1,0:T(8,128)(2,1)}), bf16[16,64,128]{2,1,0:T(8,128)(2,1)S(1)}, u32[]{:S(2)}, u32[]{:S(2)}) async-start(bf16[16,64,128]{2,1,0:T(8,128)(2,1)} %bitcast.126), calls=%async_computation.10 | async-start | bytes 524288 | tf_op jit(solution)/shard_map/all_to_all | solution.py:235
  443.9 15.1 %all-to-all-start.9 = ((bf16[16,64,128]{2,1,0:T(8,128)(2,1)}), bf16[16,64,128]{2,1,0:T(8,128)(2,1)S(1)}, u32[]{:S(2)}, u32[]{:S(2)}) async-start(bf16[16,64,128]{2,1,0:T(8,128)(2,1)} %bitcast.124), calls=%async_computation.9 | async-start | bytes 524288 | tf_op jit(solution)/shard_map/all_to_all | solution.py:234
where the time goes:
time: 461 us; the launch traced here: 460 us
  waiting for transfers between devices  197 us (43%)
  starting transfers between devices  181 us (39%)
  local copies, waits for them, and re-layouts  52.9 us (11%)
  matrix products  15.5 us (3%)
  other arithmetic  11.9 us (3%)
    ppermute x5, waiting for transfers between devices, reduce_to_first(): value = value + lax.ppermute(value, axis, pairs)  111 us
    ppermute x5, starting transfers between devices, broadcast(): got = lax.ppermute(value, axis, pairs)  84 us
    all_to_all x1, starting transfers between devices, shards(): lax.all_to_all(outgoing.reshape(2, groups, capacity, BLK, head_count, HD)...  17.6 us
    all_to_all x1, starting transfers between devices, shards(): lax.all_to_all(request_table(random_blocks, query_count, groups, capacity...  12.9 us
    all_to_all x1, waiting for transfers between devices, shards(): lax.all_to_all(values, 'head', split_axis=1, concat_axis=0, tiled=True)  11.6 us
    all_to_all x1, starting transfers between devices, shards(): lax.all_to_all(attended.reshape(group_tokens, head_count * HD), 'head', s...  10.5 us
    all_to_all x1, waiting for transfers between devices, shards(): lax.all_to_all(grad_k, 'head', split_axis=0, concat_axis=1, tiled=True)  10.2 us
    all_to_all x1, waiting for transfers between devices, shards(): lax.all_to_all(queries, 'head', split_axis=1, concat_axis=0, tiled=True)  9.99 us
  transfers between devices with their start and end apart: 25, of which 19 were waited for; matrix products, arithmetic and copies ran while one was open for 10% of the time, Pallas kernels for 0%

commit v1 on v0

--- a/solution.py
+++ b/solution.py
@@ -119,10 +119,16 @@
 def shards(queries, keys, values, grad_out, random_blocks):
     groups = lax.axis_size("seq")
     my_group = lax.axis_index("seq")
+
+    def wrap_floor(here_x):
+        return jnp.concatenate(
+            lax.all_to_all(jnp.stack(jnp.split(here_x, lax.axis_size("head"), 1)), "head", 0, 0), 0
+        )
+
     head_q, head_k, head_v, head_g = (
         lax.all_to_all(queries, "head", split_axis=1, concat_axis=0, tiled=True),
         lax.all_to_all(keys, "head", split_axis=1, concat_axis=0, tiled=True),
-        lax.all_to_all(values, "head", split_axis=1, concat_axis=0, tiled=True),
+        wrap_floor(values),
         lax.all_to_all(grad_out, "head", split_axis=1, concat_axis=0, tiled=True),
     )
     group_tokens = head_q.shape[0]

time: 461 us -> 475 us (1.030)
  local copies, waits for them, and re-layouts: 52.9 us -> 73.3 us
  waiting for transfers between devices: 197 us -> 185 us
  starting transfers between devices: 181 us -> 186 us
    unnamed x42 -> x55, local copies, waits for them, and re-layouts: 4.32 us -> 24.2 us
    all_to_all x1, waiting for transfers between devices: 6.8 us -> 0.01 us  [shards(): lax.all_to_all(request_table(random_blocks, query_count, groups, capacity...]
  transfers between devices with their start and end apart: 25 -> 25, of which waited for: 19 -> 18; matrix products, arithmetic and copies ran while one was open for 10% -> 14% of each run, Pallas kernels for 0% -> 0%
where the time goes in v1:
time: 475 us; the launch traced here: 473 us
  starting transfers between devices  186 us (39%)
  waiting for transfers between devices  185 us (39%)
  local copies, waits for them, and re-layouts  73.3 us (15%)
  matrix products  15.5 us (3%)
  other arithmetic  11.9 us (3%)
    ppermute x5, waiting for transfers between devices, reduce_to_first(): value = value + lax.ppermute(value, axis, pairs)  111 us
    ppermute x5, starting transfers between devices, broadcast(): got = lax.ppermute(value, axis, pairs)  86 us
    unnamed x55, local copies, waits for them, and re-layouts  24.2 us
    all_to_all x1, starting transfers between devices, shards(): lax.all_to_all(outgoing.reshape(2, groups, capacity, BLK, head_count, HD)...  17.3 us
    all_to_all x1, starting transfers between devices, shards(): lax.all_to_all(request_table(random_blocks, query_count, groups, capacity...  12.9 us
    all_to_all x1, waiting for transfers between devices, wrap_floor(): lax.all_to_all(jnp.stack(jnp.split(here_x, lax.axis_size('head'), 1)), 'h...  11.6 us
    all_to_all x1, starting transfers between devices, shards(): lax.all_to_all(attended.reshape(group_tokens, head_count * HD), 'head', s...  10.7 us
    all_to_all x1, waiting for transfers between devices, shards(): lax.all_to_all(grad_k, 'head', split_axis=0, concat_axis=1, tiled=True)  10.2 us
  transfers between devices with their start and end apart: 25, of which 18 were waited for; matrix products, arithmetic and copies ran while one was open for 14% of the time, Pallas kernels for 0%

profile of v1, /device:TPU:3, one launch (start us, length us, event | category | flops | bytes accessed | tf_op | source)
XLA Modules:
  0.0 472.9 jit_solution(16439823002671946422)
XLA Ops:
  2.7 12.9 %all-to-all-start.3 = ((s32[32,1,2]{2,1,0:T(1,128)}), s32[32,1,2]{2,1,0:T(1,128)S(1)}, u32[]{:S(2)}, u32[]{:S(2)}) async-start(s32[32,1,2]{2,1,0:T(1,128)} %bitcast.35), calls=%async_computation.3 | async-start | bytes 32768 | tf_op jit(solution)/shard_map/all_to_all | solution.py:150
  32.3 8.3 %all-to-all-start.2 = ((bf16[64,16,128]{2,0,1:T(8,128)(2,1)}), bf16[64,16,128]{2,0,1:T(8,128)(2,1)S(1)}, u32[]{:S(2)}, u32[]{:S(2)}) async-start(bf16[64,16,128]{2,0,1:T(8,128)(2,1)} %copy_bitcast_fusion.8), calls=%async_computation.2 | async-start | bytes 524288 | tf_op jit(solution)/shard_map/all_to_all | solution.py:129
  43.3 1.7 copy_bitcast_fusion.9
  45.0 7.3 %all-to-all-done.2 = bf16[64,16,128]{2,0,1:T(8,128)(2,1)S(1)} async-done(((bf16[64,16,128]{2,0,1:T(8,128)(2,1)}), bf16[64,16,128]{2,0,1:T(8,128)(2,1)S(1)}, u32[]{:S(2)}, u32[]{:S(2)}) %all-to-all-start.2) | async-done | bytes 262176 | tf_op jit(solution)/shard_map/all_to_all | solution.py:129
  52.3 3.4 all-to-all-start
  60.6 6.3 %all-to-all-done = bf16[64,16,128]{2,0,1:T(8,128)(2,1)S(1)} async-done(((bf16[64,16,128]{2,0,1:T(8,128)(2,1)}), bf16[64,16,128]{2,0,1:T(8,128)(2,1)S(1)}, u32[]{:S(2)}, u32[]{:S(2)}) %all-to-all-start) | async-done | bytes 262176 | tf_op jit(solution)/shard_map/all_to_all | solution.py:130
  66.9 3.4 all-to-all-start.1
  70.5 11.6 %all-to-all-done.1 = bf16[16,64,128]{2,1,0:T(8,128)(2,1)S(1)} async-done(((bf16[16,64,128]{2,1,0:T(8,128)(2,1)}), bf16[16,64,128]{2,1,0:T(8,128)(2,1)S(1)}, u32[]{:S(2)}, u32[]{:S(2)}) %all-to-all-start.1) | async-done | bytes 262176 | tf_op jit(solution)/shard_map/all_to_all | solution.py:125
  82.0 3.4 all-to-all-start.6
  85.5 3.1 gather_fusion
  88.6 2.7 copy.164
  91.8 2.5 copy.165
  94.3 2.3 all-to-all-done.6
  96.6 9.3 %all-to-all-start.4 = ((bf16[2,32,2,128,1,128]{5,3,2,0,4,1:T(8,128)(2,1)}), bf16[2,32,2,128,1,128]{5,3,2,0,4,1:T(8,128)(2,1)}, u32[]{:S(2)}, u32[]{:S(2)}) async-start(bf16[2,32,2,128,1,128]{5,3,2,0,4,1:T(8,128)(2,1)} %copy.165), calls=%async_computation.4 | async-start | bytes 8388608 | tf_op jit(solution)/shard_map/all_to_all | solution.py:159
  106.2 3.1 collective-permute-start.5
  109.3 2.2 collective-permute-start.6
  112.8 7.4 %collective-permute-done.5 = bf16[2,128,128]{2,1,0:T(8,128)(2,1)S(1)} collective-permute-done((bf16[2,128,128]{2,1,0:T(8,128)(2,1)S(1)}, bf16[2,128,128]{2,1,0:T(8,128)(2,1)S(1)}, u32[]{:S(2)}, u32[]{:S(2)}) %collective-permute-start.5) | collective-permute-done | bytes 65568 | tf_op jit(solution)/shard_map/ppermute | solution.py:19
  120.3 3.2 collective-permute-done
  123.5 80.7 %collective-permute-start.1 = (bf16[2,256,1,128]{3,1,2,0:T(8,128)(2,1)S(1)}, bf16[2,256,1,128]{3,1,2,0:T(8,128)(2,1)S(1)}, u32[]{:S(2)}, u32[]{:S(2)}) collective-permute-start(bf16[2,256,1,128]{3,1,2,0:T(8,128)(2,1)S(1)} %broadcast_select_fusion.1), channel_id=1, source_target_pairs={{0,2},{1,3},{32,34},{33,35},{64,66},{65,67},{96,98},{97,99},{128,1... | collective-permute-start | bytes 393224 | tf_op jit(solution)/shard_map/ppermute | solution.py:34
  204.6 1.6 collective-permute-done.1
  207.6 1.8 collective-permute-done.2
  211.1 1.6 collective-permute-done.3
  214.2 1.5 convolution_bitcast_fusion.1
  218.2 4.8 %copy.166 = bf16[2,32,2,128,1,128]{5,3,2,1,0,4:T(8,128)(2,1)} copy(bf16[2,32,2,128,1,128]{5,3,2,0,4,1:T(8,128)(2,1)} %all-to-all-done.4) | data formatting | bytes 8388608 | tf_op jit(solution)/shard_map/all_to_all | solution.py:159
  223.0 4.1 gather_fusion.1
  227.1 1.6 bitcast_select_fusion
  233.9 1.9 multiply_reduce_fusion
  235.9 2.3 multiply_convert_fusion
  242.1 6.7 %copy.185 = bf16[2,32,2,128,1,128]{5,2,3,0,4,1:T(2,128)(2,1)} copy(bf16[2,32,2,128,1,128]{5,2,1,3,0,4:T(2,128)(2,1)S(1)} %bitcast.335) | data formatting | bytes 8388608 | tf_op jit(solution)/shard_map/reshape | solution.py:205
  248.8 17.3 %all-to-all-start.8 = ((bf16[2,32,2,128,1,128]{5,2,3,0,4,1:T(2,128)(2,1)}), bf16[2,32,2,128,1,128]{5,2,3,0,4,1:T(2,128)(2,1)}, u32[]{:S(2)}, u32[]{:S(2)}) async-start(bf16[2,32,2,128,1,128]{5,2,3,0,4,1:T(2,128)(2,1)} %copy.185), calls=%async_computation.8 | async-start | bytes 8388608 | tf_op jit(solution)/shard_map/all_to_all | solution.py:204
  273.2 93.2 %collective-permute-done.9 = f32[2,256,1,128]{3,1,2,0:T(8,128)S(1)} collective-permute-done((f32[2,256,1,128]{3,1,2,0:T(8,128)S(1)}, f32[2,256,1,128]{3,1,2,0:T(8,128)S(1)}, u32[]{:S(2)}, u32[]{:S(2)}) %collective-permute-start.9) | collective-permute-done | bytes 262176 | tf_op jit(solution)/shard_map/ppermute | solution.py:47
  368.2 3.5 collective-permute-start.7
  371.7 1.9 collective-permute-start.8
  374.1 5.9 %collective-permute-done.10 = f32[2,256,1,128]{3,1,2,0:T(8,128)S(1)} collective-permute-done((f32[2,256,1,128]{3,1,2,0:T(8,128)S(1)}, f32[2,256,1,128]{3,1,2,0:T(8,128)S(1)}, u32[]{:S(2)}, u32[]{:S(2)}) %collective-permute-start.10) | collective-permute-done | bytes 262176 | tf_op jit(solution)/shard_map/ppermute | solution.py:47
  382.4 5.5 %collective-permute-done.11 = f32[2,256,1,128]{3,1,2,0:T(8,128)S(1)} collective-permute-done((f32[2,256,1,128]{3,1,2,0:T(8,128)S(1)}, f32[2,256,1,128]{3,1,2,0:T(8,128)S(1)}, u32[]{:S(2)}, u32[]{:S(2)}) %collective-permute-start.11) | collective-permute-done | bytes 262176 | tf_op jit(solution)/shard_map/ppermute | solution.py:47
  390.3 6.3 %collective-permute-done.12 = f32[2,256,1,128]{3,1,2,0:T(8,128)S(1)} collective-permute-done((f32[2,256,1,128]{3,1,2,0:T(8,128)S(1)}, f32[2,256,1,128]{3,1,2,0:T(8,128)S(1)}, u32[]{:S(2)}, u32[]{:S(2)}) %collective-permute-start.12) | collective-permute-done | bytes 262176 | tf_op jit(solution)/shard_map/ppermute | solution.py:47
  396.6 2.9 collective-permute-start.13
  400.4 3.0 scatter-add.11
  403.4 10.7 %all-to-all-start.5 = ((bf16[16,64,128]{2,1,0:T(8,128)(2,1)}), bf16[16,64,128]{2,1,0:T(8,128)(2,1)S(1)}, u32[]{:S(2)}, u32[]{:S(2)}) async-start(bf16[16,64,128]{2,1,0:T(8,128)(2,1)} %bitcast.60), calls=%async_computation.5 | async-start | bytes 524288 | tf_op jit(solution)/shard_map/all_to_all | solution.py:226
  414.5 9.0 %copy.186 = bf16[2,32,2,128,1,128]{5,2,1,3,0,4:T(2,128)(2,1)} copy(bf16[2,32,2,128,1,128]{5,2,3,0,4,1:T(2,128)(2,1)} %all-to-all-done.8) | data formatting | bytes 8388608 | tf_op jit(solution)/shard_map/all_to_all | solution.py:204
  423.5 2.5 all-to-all-done.5
  426.0 4.8 %all-to-all-start.7 = ((bf16[16,64,128]{2,1,0:T(8,128)(2,1)}), bf16[16,64,128]{2,1,0:T(8,128)(2,1)S(1)}, u32[]{:S(2)}, u32[]{:S(2)}) async-start(bf16[16,64,128]{2,1,0:T(8,128)(2,1)} %bitcast.82), calls=%async_computation.7 | async-start | bytes 524288 | tf_op jit(solution)/shard_map/all_to_all | solution.py:233
  430.7 2.8 fusion.7
  434.4 8.1 %all-to-all-done.7 = bf16[16,64,128]{2,1,0:T(8,128)(2,1)S(1)} async-done(((bf16[16,64,128]{2,1,0:T(8,128)(2,1)}), bf16[16,64,128]{2,1,0:T(8,128)(2,1)S(1)}, u32[]{:S(2)}, u32[]{:S(2)}) %all-to-all-start.7) | async-done | bytes 262176 | tf_op jit(solution)/shard_map/all_to_all | solution.py:233
  442.4 3.4 all-to-all-start.10
  447.4 9.6 %all-to-all-done.10 = bf16[16,64,128]{2,1,0:T(8,128)(2,1)S(1)} async-done(((bf16[16,64,128]{2,1,0:T(8,128)(2,1)}), bf16[16,64,128]{2,1,0:T(8,128)(2,1)S(1)}, u32[]{:S(2)}, u32[]{:S(2)}) %all-to-all-start.10) | async-done | bytes 262176 | tf_op jit(solution)/shard_map/all_to_all | solution.py:241
  457.0 3.4 all-to-all-start.9
  461.9 10.2 %all-to-all-done.9 = bf16[16,64,128]{2,1,0:T(8,128)(2,1)S(1)} async-done(((bf16[16,64,128]{2,1,0:T(8,128)(2,1)}), bf16[16,64,128]{2,1,0:T(8,128)(2,1)S(1)}, u32[]{:S(2)}, u32[]{:S(2)}) %all-to-all-start.9) | async-done | bytes 262176 | tf_op jit(solution)/shard_map/all_to_all | solution.py:240
  (158 shorter events, 64.5 us)
Async XLA Ops:
  0.6 15.0 %copy-start = (bf16[64,2048]{1,0:T(8,128)(2,1)S(1)}, bf16[64,2048]{1,0:T(8,128)(2,1)}, u32[]{:S(2)}) copy-start(bf16[64,2048]{1,0:T(8,128)(2,1)} %param.11) | copy-start | bytes 786436
  0.6 57.8 %copy-start.16 = (bf16[64,2048]{1,0:T(8,128)(2,1)S(1)}, bf16[64,2048]{1,0:T(8,128)(2,1)}, u32[]{:S(2)}) copy-start(bf16[64,2048]{1,0:T(8,128)(2,1)} %param.14) | copy-start | bytes 786436
  2.7 29.6 %all-to-all-start.3 = ((s32[32,1,2]{2,1,0:T(1,128)}), s32[32,1,2]{2,1,0:T(1,128)S(1)}, u32[]{:S(2)}, u32[]{:S(2)}) async-start(s32[32,1,2]{2,1,0:T(1,128)} %bitcast.35), calls=%async_computation.3 | async-start | bytes 32768 | tf_op jit(solution)/shard_map/all_to_all | solution.py:150
  32.3 20.1 %all-to-all-start.2 = ((bf16[64,16,128]{2,0,1:T(8,128)(2,1)}), bf16[64,16,128]{2,0,1:T(8,128)(2,1)S(1)}, u32[]{:S(2)}, u32[]{:S(2)}) async-start(bf16[64,16,128]{2,0,1:T(8,128)(2,1)} %copy_bitcast_fusion.8), calls=%async_computation.2 | async-start | bytes 524288 | tf_op jit(solution)/shard_map/all_to_all | solution.py:129
  52.3 14.6 %all-to-all-start = ((bf16[64,16,128]{2,0,1:T(8,128)(2,1)}), bf16[64,16,128]{2,0,1:T(8,128)(2,1)S(1)}, u32[]{:S(2)}, u32[]{:S(2)}) async-start(bf16[64,16,128]{2,0,1:T(8,128)(2,1)} %copy_bitcast_fusion.9), calls=%async_computation | async-start | bytes 524288 | tf_op jit(solution)/shard_map/all_to_all | solution.py:130
  66.9 15.1 %all-to-all-start.1 = ((bf16[16,64,128]{2,1,0:T(8,128)(2,1)}), bf16[16,64,128]{2,1,0:T(8,128)(2,1)S(1)}, u32[]{:S(2)}, u32[]{:S(2)}) async-start(bf16[16,64,128]{2,1,0:T(8,128)(2,1)} %constant_dynamic-update-slice_fusion), calls=%async_computation.1 | async-start | bytes 524288 | tf_op jit(solution)/shard_map/all_to_all | solution.py:125
  82.0 14.5 %all-to-all-start.6 = ((bf16[64,16,128]{2,0,1:T(8,128)(2,1)}), bf16[64,16,128]{2,0,1:T(8,128)(2,1)S(1)}, u32[]{:S(2)}, u32[]{:S(2)}) async-start(bf16[64,16,128]{2,0,1:T(8,128)(2,1)} %copy_bitcast_fusion.7), calls=%async_computation.6 | async-start | bytes 524288 | tf_op jit(solution)/shard_map/all_to_all | solution.py:132
  96.6 121.6 %all-to-all-start.4 = ((bf16[2,32,2,128,1,128]{5,3,2,0,4,1:T(8,128)(2,1)}), bf16[2,32,2,128,1,128]{5,3,2,0,4,1:T(8,128)(2,1)}, u32[]{:S(2)}, u32[]{:S(2)}) async-start(bf16[2,32,2,128,1,128]{5,3,2,0,4,1:T(8,128)(2,1)} %copy.165), calls=%async_computation.4 | async-start | bytes 8388608 | tf_op jit(solution)/shard_map/all_to_all | solution.py:159
  106.2 14.0 %collective-permute-start.5 = (bf16[2,128,128]{2,1,0:T(8,128)(2,1)S(1)}, bf16[2,128,128]{2,1,0:T(8,128)(2,1)S(1)}, u32[]{:S(2)}, u32[]{:S(2)}) collective-permute-start(bf16[2,128,128]{2,1,0:T(8,128)(2,1)S(1)} %get-tuple-element.58), channel_id=1, source_target_pairs={{0,1},{1,2},{2,3},{3,4},{4,5},{5,6},{6,7},{7,8},{8,9},{9,10},{10,1... | collective-permute-start | bytes 196616 | tf_op jit(solution)/shard_map/ppermute | solution.py:19
  109.3 10.9 %collective-permute-start.6 = (bf16[2,128,128]{2,1,0:T(8,128)(2,1)S(1)}, bf16[2,128,128]{2,1,0:T(8,128)(2,1)S(1)}, u32[]{:S(2)}, u32[]{:S(2)}) collective-permute-start(bf16[2,128,128]{2,1,0:T(8,128)(2,1)S(1)} %get-tuple-element.59), channel_id=1, source_target_pairs={{1,0},{2,1},{3,2},{4,3},{5,4},{6,5},{7,6},{8,7},{9,8},{10,9},{11,1... | collective-permute-start | bytes 196616 | tf_op jit(solution)/shard_map/ppermute | solution.py:21
  111.5 12.0 %collective-permute-start = (bf16[2,256,1,128]{3,1,2,0:T(8,128)(2,1)S(1)}, bf16[2,256,1,128]{3,1,2,0:T(8,128)(2,1)S(1)}, u32[]{:S(2)}, u32[]{:S(2)}) collective-permute-start(bf16[2,256,1,128]{3,1,2,0:T(8,128)(2,1)S(1)} %bitcast.371), channel_id=1, source_target_pairs={{0,1},{32,33},{64,65},{96,97},{128,129},{160,161},{192,193},{224,2... | collective-permute-start | bytes 393224 | tf_op jit(solution)/shard_map/ppermute | solution.py:34
  123.5 82.6 %collective-permute-start.1 = (bf16[2,256,1,128]{3,1,2,0:T(8,128)(2,1)S(1)}, bf16[2,256,1,128]{3,1,2,0:T(8,128)(2,1)S(1)}, u32[]{:S(2)}, u32[]{:S(2)}) collective-permute-start(bf16[2,256,1,128]{3,1,2,0:T(8,128)(2,1)S(1)} %broadcast_select_fusion.1), channel_id=1, source_target_pairs={{0,2},{1,3},{32,34},{33,35},{64,66},{65,67},{96,98},{97,99},{128,1... | collective-permute-start | bytes 393224 | tf_op jit(solution)/shard_map/ppermute | solution.py:34
  206.1 3.2 collective-permute-start.2
  207.6 8.1 %copy-start.6 = (bf16[2,8,384,1,128]{4,2,1,3,0:T(8,128)(2,1)}, bf16[2,8,384,1,128]{4,2,1,3,0:T(8,128)(2,1)S(1)}, u32[]{:S(2)}) copy-start(bf16[2,8,384,1,128]{4,2,1,3,0:T(8,128)(2,1)S(1)} %pad_maximum_fusion.1) | copy-start | bytes 4718596
  209.4 3.3 collective-permute-start.3
  212.7 3.8 collective-permute-start.4
  228.9 1.8 copy-start.10
  228.9 3.3 copy-start.12
  232.2 1.4 copy-start.8
  232.3 1.7 copy-start.9
  238.2 1.4 copy-start.2
  238.2 2.0 copy-start.4
  248.8 17.4 %copy-start.3 = (bf16[8,1,128,1024]{2,3,0,1:T(8,128)(2,1)S(1)}, bf16[8,1,128,1024]{2,3,0,1:T(8,128)(2,1)}, u32[]{:S(2)}) copy-start(bf16[8,1,128,1024]{2,3,0,1:T(8,128)(2,1)} %copy-done.2) | copy-start | bytes 6291460
  248.8 154.6 %all-to-all-start.8 = ((bf16[2,32,2,128,1,128]{5,2,3,0,4,1:T(2,128)(2,1)}), bf16[2,32,2,128,1,128]{5,2,3,0,4,1:T(2,128)(2,1)}, u32[]{:S(2)}, u32[]{:S(2)}) async-start(bf16[2,32,2,128,1,128]{5,2,3,0,4,1:T(2,128)(2,1)} %copy.185), calls=%async_computation.8 | async-start | bytes 8388608 | tf_op jit(solution)/shard_map/all_to_all | solution.py:204
  266.5 3.4 copy-start.5
  268.0 98.4 %collective-permute-start.9 = (f32[2,256,1,128]{3,1,2,0:T(8,128)S(1)}, f32[2,256,1,128]{3,1,2,0:T(8,128)S(1)}, u32[]{:S(2)}, u32[]{:S(2)}) collective-permute-start(f32[2,256,1,128]{3,1,2,0:T(8,128)S(1)} %pad_maximum_fusion.5), channel_id=1, source_target_pairs={{16,0},{17,1},{18,2},{19,3},{20,4},{21,5},{22,6},{23,7},{24,8},{25... | collective-permute-start | bytes 786440 | tf_op jit(solution)/shard_map/ppermute | solution.py:47
  270.6 1.1 copy-start.13
  270.6 1.7 copy-start.7
  272.9 94.8 %copy-start.11 = (bf16[1,24,128,1,128]{4,2,0,1,3:T(8,128)(2,1)S(1)}, bf16[1,24,128,1,128]{4,2,0,1,3:T(8,128)(2,1)}, u32[]{:S(2)}) copy-start(bf16[1,24,128,1,128]{4,2,0,1,3:T(8,128)(2,1)} %copy-done.10) | copy-start | bytes 2359300
  273.2 95.0 %copy-start.14 = (f32[2,10,128,1,128]{4,2,0,3,1:T(8,128)}, f32[2,10,128,1,128]{4,2,0,3,1:T(8,128)S(1)}, u32[]{:S(2)}) copy-start(f32[2,10,128,1,128]{4,2,0,3,1:T(8,128)S(1)} %bitcast_add_fusion) | copy-start | bytes 3932164
  366.4 13.5 %collective-permute-start.10 = (f32[2,256,1,128]{3,1,2,0:T(8,128)S(1)}, f32[2,256,1,128]{3,1,2,0:T(8,128)S(1)}, u32[]{:S(2)}, u32[]{:S(2)}) collective-permute-start(f32[2,256,1,128]{3,1,2,0:T(8,128)S(1)} %fusion.39), channel_id=1, source_target_pairs={{8,0},{9,1},{10,2},{11,3},{12,4},{13,5},{14,6},{15,7},{40,32},{41,... | collective-permute-start | bytes 786440 | tf_op jit(solution)/shard_map/ppermute | solution.py:47
  368.2 31.3 %collective-permute-start.7 = (bf16[2,128,1,128]{3,1,0,2:T(8,128)(2,1)S(1)}, bf16[2,128,1,128]{3,1,0,2:T(8,128)(2,1)S(1)}, u32[]{:S(2)}, u32[]{:S(2)}) collective-permute-start(bf16[2,128,1,128]{3,1,0,2:T(8,128)(2,1)S(1)} %get-tuple-element.49), channel_id=1, source_target_pairs={{0,1},{1,2},{2,3},{3,4},{4,5},{5,6},{6,7},{7,8},{8,9},{9,10},{10,1... | collective-permute-start | bytes 196616 | tf_op jit(solution)/shard_map/ppermute | solution.py:19
  371.7 27.8 %collective-permute-start.8 = (bf16[2,128,1,128]{3,1,0,2:T(8,128)(2,1)S(1)}, bf16[2,128,1,128]{3,1,0,2:T(8,128)(2,1)S(1)}, u32[]{:S(2)}, u32[]{:S(2)}) collective-permute-start(bf16[2,128,1,128]{3,1,0,2:T(8,128)(2,1)S(1)} %get-tuple-element.50), channel_id=1, source_target_pairs={{1,0},{2,1},{3,2},{4,3},{5,4},{6,5},{7,6},{8,7},{9,8},{10,9},{11,1... | collective-permute-start | bytes 196616 | tf_op jit(solution)/shard_map/ppermute | solution.py:21
  380.0 7.8 %collective-permute-start.11 = (f32[2,256,1,128]{3,1,2,0:T(8,128)S(1)}, f32[2,256,1,128]{3,1,2,0:T(8,128)S(1)}, u32[]{:S(2)}, u32[]{:S(2)}) collective-permute-start(f32[2,256,1,128]{3,1,2,0:T(8,128)S(1)} %fusion.61), channel_id=1, source_target_pairs={{4,0},{5,1},{6,2},{7,3},{36,32},{37,33},{38,34},{39,35},{68,64},{6... | collective-permute-start | bytes 786440 | tf_op jit(solution)/shard_map/ppermute | solution.py:47
  382.4 17.1 %copy-start.15 = (f32[2,10,128,1,128]{4,2,0,3,1:T(8,128)S(1)}, f32[2,10,128,1,128]{4,2,0,3,1:T(8,128)}, u32[]{:S(2)}) copy-start(f32[2,10,128,1,128]{4,2,0,3,1:T(8,128)} %copy-done.14) | copy-start | bytes 3932164
  382.4 17.2 %slice-start = ((f32[2,10,128,1,128]{4,2,0,3,1:T(8,128)}), f32[2,8,128,1,128]{4,2,0,3,1:T(8,128)S(1)}, s32[]{:S(2)}) async-start(f32[2,10,128,1,128]{4,2,0,3,1:T(8,128)} %copy-done.14), calls=%async_computation.11 | async-start | bytes 2097152 | tf_op jit(solution)/shard_map/slice | solution.py:190
  387.9 8.6 %collective-permute-start.12 = (f32[2,256,1,128]{3,1,2,0:T(8,128)S(1)}, f32[2,256,1,128]{3,1,2,0:T(8,128)S(1)}, u32[]{:S(2)}, u32[]{:S(2)}) collective-permute-start(f32[2,256,1,128]{3,1,2,0:T(8,128)S(1)} %add.165), channel_id=1, source_target_pairs={{2,0},{3,1},{34,32},{35,33},{66,64},{67,65},{98,96},{99,97},{130,1... | collective-permute-start | bytes 786440 | tf_op jit(solution)/shard_map/ppermute | solution.py:47
  396.6 17.6 %collective-permute-start.13 = (f32[2,256,1,128]{3,1,2,0:T(8,128)S(1)}, f32[2,256,1,128]{3,1,2,0:T(8,128)S(1)}, u32[]{:S(2)}, u32[]{:S(2)}) collective-permute-start(f32[2,256,1,128]{3,1,2,0:T(8,128)S(1)} %add.166), channel_id=1, source_target_pairs={{1,0},{33,32},{65,64},{97,96},{129,128},{161,160},{193,192},{225,2... | collective-permute-start | bytes 786440 | tf_op jit(solution)/shard_map/ppermute | solution.py:47
  403.4 22.6 %all-to-all-start.5 = ((bf16[16,64,128]{2,1,0:T(8,128)(2,1)}), bf16[16,64,128]{2,1,0:T(8,128)(2,1)S(1)}, u32[]{:S(2)}, u32[]{:S(2)}) async-start(bf16[16,64,128]{2,1,0:T(8,128)(2,1)} %bitcast.60), calls=%async_computation.5 | async-start | bytes 524288 | tf_op jit(solution)/shard_map/all_to_all | solution.py:226
  426.0 16.5 %all-to-all-start.7 = ((bf16[16,64,128]{2,1,0:T(8,128)(2,1)}), bf16[16,64,128]{2,1,0:T(8,128)(2,1)S(1)}, u32[]{:S(2)}, u32[]{:S(2)}) async-start(bf16[16,64,128]{2,1,0:T(8,128)(2,1)} %bitcast.82), calls=%async_computation.7 | async-start | bytes 524288 | tf_op jit(solution)/shard_map/all_to_all | solution.py:233
  433.6 39.3 %copy-start.1 = (bf16[64,2048]{1,0:T(8,128)(2,1)S(1)}, bf16[64,2048]{1,0:T(8,128)(2,1)}, u32[]{:S(2)}) copy-start(bf16[64,2048]{1,0:T(8,128)(2,1)} %param.11) | copy-start | bytes 786436
  442.4 14.6 %all-to-all-start.10 = ((bf16[16,64,128]{2,1,0:T(8,128)(2,1)}), bf16[16,64,128]{2,1,0:T(8,128)(2,1)S(1)}, u32[]{:S(2)}, u32[]{:S(2)}) async-start(bf16[16,64,128]{2,1,0:T(8,128)(2,1)} %bitcast.141), calls=%async_computation.10 | async-start | bytes 524288 | tf_op jit(solution)/shard_map/all_to_all | solution.py:241
  457.0 15.1 %all-to-all-start.9 = ((bf16[16,64,128]{2,1,0:T(8,128)(2,1)}), bf16[16,64,128]{2,1,0:T(8,128)(2,1)S(1)}, u32[]{:S(2)}, u32[]{:S(2)}) async-start(bf16[16,64,128]{2,1,0:T(8,128)(2,1)} %bitcast.139), calls=%async_computation.9 | async-start | bytes 524288 | tf_op jit(solution)/shard_map/all_to_all | solution.py:240
